TPU v7x, 32 devices: a whole 2x2x4 slice. The times are simulated.
32 devices in a mesh: amp: 8 (over y, x, core), int: 4 (over z).
Axes of the slice: x: 2, y: 2, z: 4, core: 2. Of those that a mesh axis runs over, the one named last changes fastest.
Arguments:
- amplitudes: float32 [768, 512], P('int'), may hold values from -6 to 6
- slab_integrals: float32 [512, 51200], P('int', 'amp'), may hold values from -0.25 to 0.25
- cycle_integrals: float32 [96, 800, 512], P('int', 'amp'), may hold values from -0.03125 to 0.03125
- occ_irrep: int32 [96], replicated, may hold values from 0 to 7
- vir_irrep: int32 [800], replicated, may hold values from 0 to 7
Outputs:
- ladder: float32 [768, 51200], P('int', 'amp')
- cycle: float32 [512, 512], P('int', 'amp')
All inputs are finite; a program needn't handle non-finite values.
Results may differ from a plain program's by a relative error of at most 0.00011.
Values sent between devices are 32-bit elements; how exact they have to be, the bound alone decides.
No kernel may reach another device: no remote copies, remote signals or barrier semaphores. Data moves between devices by JAX's collectives and lax.ppermute only.
A program may use at most 64 MiB of HBM per device.

v0:
```python
import jax
import jax.numpy as jnp
from jax import lax
from jax.sharding import PartitionSpec as P

PRECISION = lax.Precision.HIGH


def per_device(amplitudes, slab_integrals, cycle_integrals, occ_irrep, vir_irrep, n_amp, n_int):
    nocc = occ_irrep.shape[0]
    nvir = vir_irrep.shape[0]
    rows, pw = amplitudes.shape
    pw_local = slab_integrals.shape[0]
    i_local = rows // nocc
    ibat = i_local * n_int
    width = slab_integrals.shape[1]
    a_local = width // nvir
    slab = a_local * n_amp
    k_local, c_local, columns = cycle_integrals.shape
    if a_local >= 4:
        sizes = [(a_local - 1) // 2, a_local - 2 - (a_local - 1) // 2, 1, 1]
    elif a_local >= 2:
        sizes = [a_local - 1, 1]
    else:
        sizes = [a_local]
    chunks = len(sizes)
    starts = [sum(sizes[:t]) for t in range(chunks)]
    t_cyc = lax.all_to_all(
        amplitudes.reshape(i_local, nocc, pw), "int", split_axis=1, concat_axis=0, tiled=True
    ).reshape(ibat * k_local, pw)
    w2 = cycle_integrals.transpose(1, 0, 2).reshape(c_local * k_local, columns)
    ladder_chunks = []
    cycle_chunks = []
    for t in range(chunks):
        a_chunk = sizes[t]
        v = lax.slice_in_dim(slab_integrals, starts[t] * nvir, (starts[t] + a_chunk) * nvir, axis=1)
        v_all = lax.all_gather(v, "int", axis=0, tiled=True)
        if t:
            v_all, ladder_chunks[-1], cycle_chunks[-1] = lax.optimization_barrier(
                (v_all, ladder_chunks[-1], cycle_chunks[-1])
            )
        ladder_chunks.append(
            jnp.dot(amplitudes, v_all, precision=PRECISION, preferred_element_type=jnp.float32)
        )
        l_cyc = jnp.dot(t_cyc, v_all, precision=PRECISION, preferred_element_type=jnp.float32)
        l_cyc = l_cyc.reshape(ibat, k_local, a_chunk, n_amp, c_local).transpose(3, 0, 2, 4, 1)
        l_cyc = l_cyc.reshape(n_amp, ibat * a_chunk, c_local * k_local)
        moved = lax.all_to_all(l_cyc, "amp", split_axis=0, concat_axis=0, tiled=True)
        moved = moved.reshape(n_amp * ibat * a_chunk, c_local * k_local)
        cycle_chunks.append(
            jnp.dot(moved, w2, precision=PRECISION, preferred_element_type=jnp.float32)
        )
    ladder = jnp.concatenate(ladder_chunks, axis=1)
    parts = jnp.concatenate(
        [c.reshape(n_amp, ibat, sizes[t], columns) for t, c in enumerate(cycle_chunks)], axis=2
    )
    col_local = columns // n_amp
    parts = parts.transpose(1, 0, 2, 3).reshape(n_int, i_local * slab, n_amp, col_local)
    parts = parts.transpose(0, 2, 1, 3).reshape(n_int * n_amp, i_local * slab, col_local)
    gathered = lax.all_to_all(parts, ("int", "amp"), split_axis=0, concat_axis=0, tiled=True)
    sums = jnp.sum(gathered, axis=0)
    row_start = lax.axis_index("int") * i_local
    batch_labels = lax.dynamic_slice_in_dim(occ_irrep, row_start, i_local, 0)
    slab_labels = vir_irrep[:slab]
    row_labels = jnp.bitwise_xor(batch_labels[:, None], slab_labels[None, :]).reshape(-1)
    col_ids = lax.axis_index("amp") * col_local + jnp.arange(col_local, dtype=jnp.int32)
    col_occ = col_ids // slab
    col_vir = col_ids % slab
    occ_match = col_occ[:, None] == jnp.arange(nocc, dtype=jnp.int32)[None, :]
    vir_match = col_vir[:, None] == jnp.arange(slab, dtype=jnp.int32)[None, :]
    occ_lookup = jnp.sum(jnp.where(occ_match, occ_irrep[None, :], 0), axis=1)
    vir_lookup = jnp.sum(jnp.where(vir_match, slab_labels[None, :], 0), axis=1)
    col_labels = jnp.bitwise_xor(occ_lookup, vir_lookup)
    keep = row_labels[:, None] == col_labels[None, :]
    cycle = jnp.where(keep, sums, jnp.zeros_like(sums))
    return (ladder, cycle)


def solution(mesh):
    n_amp = mesh.shape["amp"]
    n_int = mesh.shape["int"]
    in_specs = (P("int", None), P("int", "amp"), P("int", "amp", None), P(), P())
    out_specs = (P("int", "amp"), P("int", "amp"))

    def body(*args):
        return per_device(*args, n_amp=n_amp, n_int=n_int)

    return jax.shard_map(body, mesh=mesh, in_specs=in_specs, out_specs=out_specs, check_vma=False)
```

profile of v0, /device:TPU:0, one launch (start us, length us, event | category | flops | bytes accessed | tf_op | source)
XLA Modules:
  0.0 353.6 jit_solution(3028213121475945152)
XLA Ops:
  7.2 3.6 %fusion.3 = (f32[128,2400]{1,0:T(8,128)}, f32[128,2400]{1,0:T(8,128)}) fusion(f32[128,6400]{1,0:T(8,128)} %param.6), kind=kLoop, calls=%fused_computation.24 | loop fusion | bytes 4915200 | tf_op jit(solution)/shard_map/slice | solution.py:36
  10.9 0.7 all-gather.5.cloned.1.call-update
  12.1 27.5 %all_to_all.40 = f32[2,96,512]{2,0,1:T(2,128)S(1)} all-to-all(f32[2,96,512]{2,0,1:T(2,128)S(1)} %copy.57), channel_id=1, replica_groups=mesh['amp'=8,'int'=4] {'int'}, dimensions={1} | all-to-all | bytes 786432 | tf_op jit(solution)/shard_map/all_to_all | solution.py:28
  39.7 71.0 %all-gather.7.cloned.1.call-done = f32[512,2400]{1,0:T(8,128)} async-done(((f32[128,2400]{1,0:T(8,128)}), f32[512,2400]{1,0:T(8,128)}) %all-gather.7.cloned.1.call-update) | async-done | bytes 4915216 | tf_op jit(solution)/shard_map/all_gather | solution.py:37
  110.7 5.7 %copy.60 = f32[2400,512]{1,0:T(8,128)} copy(f32[2400,512]{0,1:T(8,128)} %bitcast.79) | data formatting | bytes 9830400 | tf_op jit(solution)/shard_map/dot_general | solution.py:45
  116.4 5.4 %reshape.144 = f32[3,8,100,512,1]{3,2,1,0,4:T(8,128)} reshape(f32[2400,512]{1,0:T(8,128)} %copy.60) | data formatting | bytes 9830400 | tf_op jit(solution)/shard_map/dot_general | solution.py:45
  121.9 4.9 %convolution_bitcast_fusion.2 = f32[8,8,3,100,24]{3,4,0,2,1:T(8,128)S(1)} fusion(f32[8,24,512,1,1]{2,1,4,3,0:T(8,128)S(1)} %bitcast.82, f32[3,8,100,512,1]{3,2,1,0,4:T(8,128)} %reshape.144), kind=kOutput, calls=%fused_computation.2 | convolution fusion | flops 1415577600 | bytes 7151616 | tf_op jit(solution)/shard_map/dot_general | solution.py:45
  126.8 5.6 %copy.61 = f32[8,8,3,100,24]{4,3,2,1,0:T(8,128)} copy(f32[8,8,3,100,24]{3,4,0,2,1:T(8,128)S(1)} %convolution_bitcast_fusion.2) | data formatting | bytes 3686400 | tf_op jit(solution)/shard_map/transpose | solution.py:46
  132.5 7.6 %reshape.126 = f32[8,24,2400]{2,1,0:T(8,128)} reshape(f32[8,8,3,100,24]{4,3,2,1,0:T(8,128)} %copy.61) | data formatting | bytes 3686400 | tf_op jit(solution)/shard_map/reshape | solution.py:47
  140.1 3.8 %all-to-all-start.1 = ((f32[8,24,2400]{2,1,0:T(8,128)}), f32[8,24,2400]{2,1,0:T(8,128)S(1)}, u32[]{:S(2)}, u32[]{:S(2)}) async-start(f32[8,24,2400]{2,1,0:T(8,128)} %reshape.126), calls=%async_computation.1 | async-start | bytes 3735552 | tf_op jit(solution)/shard_map/all_to_all | solution.py:48
  144.1 2.5 fusion.2
  146.6 5.6 %fusion.4 = f32[192,2400]{1,0:T(8,128)} fusion(f32[192,512]{1,0:T(8,128)S(1)} %copy-done.2, f32[512,2400]{1,0:T(8,128)} %all-gather.7.cloned.1.call-done), kind=kOutput, calls=%fused_computation.25 | convolution fusion | flops 1415577600 | bytes 7151616 | tf_op jit(solution)/shard_map/dot_general | solution.py:43
  152.2 15.8 %all-to-all-done.1 = f32[8,24,2400]{2,1,0:T(8,128)S(1)} async-done(((f32[8,24,2400]{2,1,0:T(8,128)}), f32[8,24,2400]{2,1,0:T(8,128)S(1)}, u32[]{:S(2)}, u32[]{:S(2)}) %all-to-all-start.1) | async-done | bytes 1843232 | tf_op jit(solution)/shard_map/all_to_all | solution.py:48
  168.0 5.1 %fusion.5 = f32[192,512]{1,0:T(8,128)} fusion(f32[192,2400]{1,0:T(8,128)S(1)} %bitcast.88, f32[2400,512]{1,0:T(8,128)} %bitcast.74), kind=kOutput, calls=%fused_computation.26 | convolution fusion | flops 1415577600 | bytes 7151616 | tf_op jit(solution)/shard_map/dot_general | solution.py:51
  173.2 32.0 %all-gather.5.cloned.1.call-done = f32[512,2400]{1,0:T(8,128)} async-done(((f32[128,2400]{1,0:T(8,128)}), f32[512,2400]{1,0:T(8,128)}) %all-gather.5.cloned.1.call-update) | async-done | bytes 4915216 | tf_op jit(solution)/shard_map/all_gather | solution.py:37
  205.2 5.5 %convolution_bitcast_fusion = f32[192,2400]{1,0:T(8,128)} fusion(f32[512,2400]{1,0:T(8,128)} %all-gather.5.cloned.1.call-done, f32[192,512]{1,0:T(8,128)S(1)} %bitcast.83), kind=kOutput, calls=%fused_computation | convolution fusion | flops 1415577600 | bytes 7151616 | tf_op jit(solution)/shard_map/dot_general | solution.py:45
  210.6 2.6 reshape.130
  213.3 5.6 %copy.63 = f32[8,24,3,8,100]{1,4,2,0,3:T(8,128)} copy(f32[8,24,3,8,100]{4,3,2,1,0:T(8,128)S(1)} %reshape.130) | data formatting | bytes 3686400 | tf_op jit(solution)/shard_map/reshape | solution.py:46
  218.9 7.6 %reshape.131 = f32[8,24,2400]{2,1,0:T(8,128)} reshape(f32[8,8,3,100,24]{4,3,2,1,0:T(8,128)} %bitcast.78) | data formatting | bytes 3686400 | tf_op jit(solution)/shard_map/reshape | solution.py:47
  226.5 3.6 %all-to-all-start.2 = ((f32[8,24,2400]{2,1,0:T(8,128)}), f32[8,24,2400]{2,1,0:T(8,128)S(1)}, u32[]{:S(2)}, u32[]{:S(2)}) async-start(f32[8,24,2400]{2,1,0:T(8,128)} %reshape.131), calls=%async_computation.2 | async-start | bytes 3735552 | tf_op jit(solution)/shard_map/all_to_all | solution.py:48
  230.6 5.5 %convolution_bitcast_fusion.1 = f32[192,2400]{1,0:T(8,128)} fusion(f32[512,2400]{1,0:T(8,128)} %all-gather.5.cloned.1.call-done, f32[192,512]{1,0:T(8,128)S(1)} %copy-done.2), kind=kOutput, calls=%fused_computation.1 | convolution fusion | flops 1415577600 | bytes 7151616 | tf_op jit(solution)/shard_map/dot_general | solution.py:43
  236.1 18.1 %all-to-all-done.2 = f32[8,24,2400]{2,1,0:T(8,128)S(1)} async-done(((f32[8,24,2400]{2,1,0:T(8,128)}), f32[8,24,2400]{2,1,0:T(8,128)S(1)}, u32[]{:S(2)}, u32[]{:S(2)}) %all-to-all-start.2) | async-done | bytes 1843232 | tf_op jit(solution)/shard_map/all_to_all | solution.py:48
  254.3 5.2 %fusion.6 = f32[192,512]{1,0:T(8,128)} fusion(f32[192,2400]{1,0:T(8,128)S(1)} %bitcast.89, f32[2400,512]{1,0:T(8,128)} %bitcast.75), kind=kOutput, calls=%fused_computation.27 | convolution fusion | flops 1415577600 | bytes 7151616 | tf_op jit(solution)/shard_map/dot_general | solution.py:51
  259.5 2.3 convolution_bitcast_fusion.5
  261.8 1.3 reshape.133
  263.1 2.2 copy.64
  265.3 1.7 reshape.134
  267.1 3.5 %all-to-all-start.3 = ((f32[8,8,2400]{2,1,0:T(8,128)}), f32[8,8,2400]{2,1,0:T(8,128)S(1)}, u32[]{:S(2)}, u32[]{:S(2)}) async-start(f32[8,8,2400]{2,1,0:T(8,128)} %reshape.134), calls=%async_computation.3 | async-start | bytes 1245184 | tf_op jit(solution)/shard_map/all_to_all | solution.py:48
  270.6 3.2 convolution_bitcast_fusion.6
  273.8 7.5 %all-to-all-done.3 = f32[8,8,2400]{2,1,0:T(8,128)S(1)} async-done(((f32[8,8,2400]{2,1,0:T(8,128)}), f32[8,8,2400]{2,1,0:T(8,128)S(1)}, u32[]{:S(2)}, u32[]{:S(2)}) %all-to-all-start.3) | async-done | bytes 614432 | tf_op jit(solution)/shard_map/all_to_all | solution.py:48
  281.3 4.0 %fusion = f32[64,512]{1,0:T(8,128)S(1)} fusion(f32[2400,512]{1,0:T(8,128)} %bitcast.76, f32[8,8,2400]{2,1,0:T(8,128)S(1)} %all-to-all-done.3), kind=kOutput, calls=%fused_computation.9 | convolution fusion | flops 471859200 | bytes 5660672 | tf_op jit(solution)/shard_map/dot_general | solution.py:51
  285.4 3.0 all-gather.11.cloned.1.call-done
  288.3 2.3 convolution_bitcast_fusion.3
  290.7 1.3 reshape.139
  292.0 2.2 copy.65
  294.2 1.7 reshape.140
  295.9 3.9 %all-to-all-start.4 = ((f32[8,8,2400]{2,1,0:T(8,128)}), f32[8,8,2400]{2,1,0:T(8,128)S(1)}, u32[]{:S(2)}, u32[]{:S(2)}) async-start(f32[8,8,2400]{2,1,0:T(8,128)} %reshape.140), calls=%async_computation.4 | async-start | bytes 1245184 | tf_op jit(solution)/shard_map/all_to_all | solution.py:48
  299.9 1.2 reshape.136
  301.3 9.2 %all-to-all-done.4 = f32[8,8,2400]{2,1,0:T(8,128)S(1)} async-done(((f32[8,8,2400]{2,1,0:T(8,128)}), f32[8,8,2400]{2,1,0:T(8,128)S(1)}, u32[]{:S(2)}, u32[]{:S(2)}) %all-to-all-start.4) | async-done | bytes 614432 | tf_op jit(solution)/shard_map/all_to_all | solution.py:48
  310.5 4.0 %convolution_bitcast_fusion.7 = f32[8,8,1,512]{3,1,0,2:T(8,128)S(1)} fusion(f32[8,8,2400]{2,1,0:T(8,128)S(1)} %all-to-all-done.4, f32[2400,512,1]{1,0,2:T(8,128)} %bitcast.77), kind=kOutput, calls=%fused_computation.7 | convolution fusion | flops 471859200 | bytes 5660672 | tf_op jit(solution)/shard_map/dot_general | solution.py:51
  314.7 0.5 maximum_bitcast_fusion
  315.7 1.6 copy.69
  317.3 2.8 all-to-all-start.5
  320.1 0.7 slice.19
  321.4 3.2 convolution_bitcast_fusion.4
  324.6 6.0 %concatenate.6 = f32[192,6400]{1,0:T(8,128)} concatenate(f32[192,2400]{1,0:T(8,128)S(1)} %copy-done.4, f32[192,2400]{1,0:T(8,128)} %convolution_bitcast_fusion.1, f32[192,800]{1,0:T(8,128)} %convolution_bitcast_fusion.6, f32[192,800]{1,0:T(8,128)} %convolution_bitcast_fusion.4), dimensions={1} | concatenate | bytes 9830400 | tf_op jit(solution)/shard_map/concatenate | solution.py:53
  330.6 15.7 %all-to-all-done.5 = f32[32,128,64]{1,2,0:T(8,128)S(1)} async-done(((f32[32,128,64]{1,2,0:T(8,128)}), f32[32,128,64]{1,2,0:T(8,128)S(1)}, u32[]{:S(2)}, u32[]{:S(2)}) %all-to-all-start.5) | async-done | bytes 1048608 | tf_op jit(solution)/shard_map/all_to_all | solution.py:60
  346.4 0.7 compare_select_fusion
  (38 shorter events, 3.2 us)
Async XLA Ops:
  7.2 103.6 %all-gather.7.cloned.1.call-start = ((), (), s32[]{:S(2)}) async-start(), calls=%async_computation.7 | async-start | bytes 6225920 | tf_op jit(solution)/shard_map/all_gather | solution.py:37
  10.8 1.0 copy-start.2
  10.8 194.3 %all-gather.5.cloned.1.call-start = ((), (), s32[]{:S(2)}) async-start(), calls=%async_computation.6 | async-start | bytes 6225920 | tf_op jit(solution)/shard_map/all_gather | solution.py:37
  39.7 219.8 %copy-start = (f32[4,2,24,512]{3,2,1,0:T(8,128)}, f32[4,2,24,512]{3,2,1,0:T(8,128)S(1)}, u32[]{:S(2)}) copy-start(f32[4,2,24,512]{3,2,1,0:T(8,128)S(1)} %copy.59) | copy-start | bytes 1179652
  140.1 28.0 %all-to-all-start.1 = ((f32[8,24,2400]{2,1,0:T(8,128)}), f32[8,24,2400]{2,1,0:T(8,128)S(1)}, u32[]{:S(2)}, u32[]{:S(2)}) async-start(f32[8,24,2400]{2,1,0:T(8,128)} %reshape.126), calls=%async_computation.1 | async-start | bytes 3735552 | tf_op jit(solution)/shard_map/all_to_all | solution.py:48
  143.9 115.6 %all-gather.9.cloned.1.call-start = ((), (), s32[]{:S(2)}) async-start(), calls=%async_computation.8 | async-start | bytes 2293760 | tf_op jit(solution)/shard_map/all_gather | solution.py:37
  226.5 27.8 %all-to-all-start.2 = ((f32[8,24,2400]{2,1,0:T(8,128)}), f32[8,24,2400]{2,1,0:T(8,128)S(1)}, u32[]{:S(2)}, u32[]{:S(2)}) async-start(f32[8,24,2400]{2,1,0:T(8,128)} %reshape.131), calls=%async_computation.2 | async-start | bytes 3735552 | tf_op jit(solution)/shard_map/all_to_all | solution.py:48
  230.1 58.3 %all-gather.11.cloned.1.call-start = ((), (), s32[]{:S(2)}) async-start(), calls=%async_computation.9 | async-start | bytes 2293760 | tf_op jit(solution)/shard_map/all_gather | solution.py:37
  267.1 14.3 %all-to-all-start.3 = ((f32[8,8,2400]{2,1,0:T(8,128)}), f32[8,8,2400]{2,1,0:T(8,128)S(1)}, u32[]{:S(2)}, u32[]{:S(2)}) async-start(f32[8,8,2400]{2,1,0:T(8,128)} %reshape.134), calls=%async_computation.3 | async-start | bytes 1245184 | tf_op jit(solution)/shard_map/all_to_all | solution.py:48
  273.8 14.5 %copy-start.1 = (f32[4,2,24,512]{3,2,1,0:T(8,128)S(1)}, f32[4,2,24,512]{3,2,1,0:T(8,128)}, u32[]{:S(2)}) copy-start(f32[4,2,24,512]{3,2,1,0:T(8,128)} %copy-done) | copy-start | bytes 1179652
  295.9 5.1 %copy-start.5 = (f32[192,512]{1,0:T(8,128)S(1)}, f32[192,512]{1,0:T(8,128)}, u32[]{:S(2)}) copy-start(f32[192,512]{1,0:T(8,128)} %fusion.6) | copy-start | bytes 1179652
  295.9 14.6 %all-to-all-start.4 = ((f32[8,8,2400]{2,1,0:T(8,128)}), f32[8,8,2400]{2,1,0:T(8,128)S(1)}, u32[]{:S(2)}, u32[]{:S(2)}) async-start(f32[8,8,2400]{2,1,0:T(8,128)} %reshape.140), calls=%async_computation.4 | async-start | bytes 1245184 | tf_op jit(solution)/shard_map/all_to_all | solution.py:48
  315.7 5.1 %copy-start.6 = (s32[96]{0:T(128)S(1)}, s32[96]{0:T(128)}, u32[]{:S(2)}) copy-start(s32[96]{0:T(128)} %param.8) | copy-start | bytes 1156
  315.7 5.7 %copy-start.3 = (f32[192,512]{1,0:T(8,128)S(1)}, f32[192,512]{1,0:T(8,128)}, u32[]{:S(2)}) copy-start(f32[192,512]{1,0:T(8,128)} %param.5) | copy-start | bytes 1179652
  317.3 7.3 %copy-start.4 = (f32[192,2400]{1,0:T(8,128)S(1)}, f32[192,2400]{1,0:T(8,128)}, u32[]{:S(2)}) copy-start(f32[192,2400]{1,0:T(8,128)} %fusion.4) | copy-start | bytes 5529604
  317.3 29.0 %all-to-all-start.5 = ((f32[32,128,64]{1,2,0:T(8,128)}), f32[32,128,64]{1,2,0:T(8,128)S(1)}, u32[]{:S(2)}, u32[]{:S(2)}) async-start(f32[32,128,64]{1,2,0:T(8,128)} %bitcast.30), calls=%async_computation.5 | async-start | bytes 2097152 | tf_op jit(solution)/shard_map/all_to_all | solution.py:60
Sparse Core Ops, SparseCore 0:
  11.0 99.7 all-gather.6
  112.3 92.8 all-gather.4
  206.8 39.7 all-gather.8
  248.0 40.2 all-gather.10
where the time goes:
time: 355 us; the launch traced here: 354 us
  waiting for transfers between devices  173 us (49%)
  local copies, waits for them, and re-layouts  68 us (19%)
  matrix products  50.8 us (14%)
  blocking collectives  27.5 us (8%)
  starting transfers between devices  18.2 us (5%)
  between operations  14 us (4%)
    all_gather x4, waiting for transfers between devices, per_device(): v_all = lax.all_gather(v, 'int', axis=0, tiled=True)  106 us
    all_to_all x4, waiting for transfers between devices, per_device(): lax.all_to_all(l_cyc, 'amp', split_axis=0, concat_axis=0, tiled=True)  50.6 us
    all_to_all x1, blocking collectives, per_device(): lax.all_to_all(amplitudes.reshape(i_local, nocc, pw), 'int', split_axis=1...  27.5 us
    reshape x4, local copies, waits for them, and re-layouts, per_device(): l_cyc = l_cyc.reshape(n_amp, ibat * a_chunk, c_local * k_local)  18.7 us
    dot_general x4, matrix products, per_device(): jnp.dot(moved, w2, precision=PRECISION, preferred_element_type=jnp.float32)  18.4 us
    dot_general x4, matrix products, per_device(): jnp.dot(amplitudes, v_all, precision=PRECISION, preferred_element_type=jn...  17.4 us
    all_to_all x1, waiting for transfers between devices, per_device(): lax.all_to_all(parts, ('int', 'amp'), split_axis=0, concat_axis=0, tiled=...  15.7 us
    reshape x6, local copies, waits for them, and re-layouts, per_device(): l_cyc.reshape(ibat, k_local, a_chunk, n_amp, c_local)  15.3 us
  transfers between devices with their start and end apart: 9, of which 8 were waited for; matrix products, arithmetic and copies ran while one was open for 29% of the time, Pallas kernels for 0%

commit v1 on v0

--- a/solution.py
+++ b/solution.py
@@ -2,6 +2,7 @@
 import jax.numpy as jnp
 from jax import lax
 from jax.sharding import PartitionSpec as P
+from jax.lax import axis_index, axis_size, ppermute
 
 PRECISION = lax.Precision.HIGH
 
@@ -34,7 +35,24 @@
     for t in range(chunks):
         a_chunk = sizes[t]
         v = lax.slice_in_dim(slab_integrals, starts[t] * nvir, (starts[t] + a_chunk) * nvir, axis=1)
-        v_all = lax.all_gather(v, "int", axis=0, tiled=True)
+
+        def save_strings_over_axis(array_axis, field):
+            shelf = []
+            slots = axis_size("int")
+            s = 0
+            while s < slots:
+                shelf.append((s, (s + 1) % slots))
+                s = s + 1
+            out_arr = [None] * slots
+            out_arr[slots - 1] = field
+            for ix in range(slots - 2, -1, -1):
+                out_arr[ix] = ppermute(out_arr[ix + 1], axis_name="int", perm=shelf)
+            z_new = jnp.concatenate(out_arr, axis=array_axis)
+            return jnp.roll(
+                z_new, (axis_index("int") + 1) * field.shape[array_axis], axis=array_axis
+            )
+
+        v_all = save_strings_over_axis(0, v)
         if t:
             v_all, ladder_chunks[-1], cycle_chunks[-1] = lax.optimization_barrier(
                 (v_all, ladder_chunks[-1], cycle_chunks[-1])

time: 355 us -> 396 us (1.12); the launches traced: 354 us -> 388 us
  waiting for transfers between devices: 173 us -> 213 us
  blocking collectives: 27.5 us -> 0 us
  other arithmetic: 1.68 us -> 19 us
  starting transfers between devices: 18.2 us -> 32.8 us
  between operations: 14 us -> 1.23 us
  local copies, waits for them, and re-layouts: 68 us -> 74.4 us
    ppermute x0 -> x12, waiting for transfers between devices: none -> 122 us  [save_strings_over_axis(): out_arr[ix] = ppermute(out_arr[ix + 1], axis_name='int', perm=shelf)]
    all_gather x4 -> x0, waiting for transfers between devices: 106 us -> none  [per_device(): v_all = lax.all_gather(v, 'int', axis=0, tiled=True)]
    all_to_all x0 -> x1, waiting for transfers between devices: none -> 54 us  [per_device(): lax.all_to_all(amplitudes.reshape(i_local, nocc, pw), 'int', split_axis=1...]
    all_to_all x4, waiting for transfers between devices: 50.6 us -> 19.9 us  [per_device(): lax.all_to_all(l_cyc, 'amp', split_axis=0, concat_axis=0, tiled=True)]
    all_to_all x1 -> x0, blocking collectives: 27.5 us -> none  [per_device(): lax.all_to_all(amplitudes.reshape(i_local, nocc, pw), 'int', split_axis=1...]
    concatenate x0 -> x4, other arithmetic: none -> 17.3 us  [save_strings_over_axis(): jnp.roll(z_new, (axis_index('int') + 1) * field.shape[array_axis], axis=a...]
    reshape x6 -> x8, local copies, waits for them, and re-layouts: 15.3 us -> 29.1 us  [per_device(): l_cyc.reshape(ibat, k_local, a_chunk, n_amp, c_local)]
    dot_general x2 -> x0, local copies, waits for them, and re-layouts: 11.1 us -> none  [per_device(): jnp.dot(t_cyc, v_all, precision=PRECISION, preferred_element_type=jnp.flo...]
  transfers between devices with their start and end apart: 9 -> 18, of which waited for: 8 -> 12; matrix products, arithmetic and copies ran while one was open for 29% -> 29% of each run, Pallas kernels for 0% -> 0%
where the time goes in v1:
time: 396 us; the launch traced here: 388 us
  waiting for transfers between devices  213 us (54%)
  local copies, waits for them, and re-layouts  74.4 us (19%)
  matrix products  47.6 us (12%)
  starting transfers between devices  32.8 us (8%)
  other arithmetic  19 us (5%)
    ppermute x12, waiting for transfers between devices, save_strings_over_axis(): out_arr[ix] = ppermute(out_arr[ix + 1], axis_name='int', perm=shelf)  122 us
    all_to_all x1, waiting for transfers between devices, per_device(): lax.all_to_all(amplitudes.reshape(i_local, nocc, pw), 'int', split_axis=1...  54 us
    reshape x8, local copies, waits for them, and re-layouts, per_device(): l_cyc.reshape(ibat, k_local, a_chunk, n_amp, c_local)  29.1 us
    reshape x4, local copies, waits for them, and re-layouts, per_device(): l_cyc = l_cyc.reshape(n_amp, ibat * a_chunk, c_local * k_local)  20.1 us
    all_to_all x4, waiting for transfers between devices, per_device(): lax.all_to_all(l_cyc, 'amp', split_axis=0, concat_axis=0, tiled=True)  19.9 us
    dot_general x4, matrix products, per_device(): jnp.dot(moved, w2, precision=PRECISION, preferred_element_type=jnp.float32)  19.6 us
    dot_general x4, matrix products, per_device(): jnp.dot(amplitudes, v_all, precision=PRECISION, preferred_element_type=jn...  17.9 us
    concatenate x4, other arithmetic, save_strings_over_axis(): jnp.roll(z_new, (axis_index('int') + 1) * field.shape[array_axis], axis=a...  17.3 us
  transfers between devices with their start and end apart: 18, of which 12 were waited for; matrix products, arithmetic and copies ran while one was open for 29% of the time, Pallas kernels for 0%

profile of v1, /device:TPU:0, one launch (start us, length us, event | category | flops | bytes accessed | tf_op | source)
XLA Modules:
  0.0 388.1 jit_solution(4929753496661729055)
XLA Ops:
  0.6 2.1 fusion.31
  4.2 3.0 collective-permute-start.3
  9.2 28.1 %collective-permute-done.3 = f32[128,2400]{0,1:T(8,128)} collective-permute-done((f32[128,2400]{0,1:T(8,128)}, f32[128,2400]{0,1:T(8,128)}, u32[]{:S(2)}, u32[]{:S(2)}) %collective-permute-start.3) | collective-permute-done | bytes 1228832 | tf_op jit(solution)/shard_map/ppermute | solution.py:49
  37.4 26.3 %collective-permute-done = f32[128,2400]{0,1:T(8,128)} collective-permute-done((f32[128,2400]{0,1:T(8,128)S(1)}, f32[128,2400]{0,1:T(8,128)}, u32[]{:S(2)}, u32[]{:S(2)}) %collective-permute-start) | collective-permute-done | bytes 1228832 | tf_op jit(solution)/shard_map/ppermute | solution.py:49
  63.7 26.3 %collective-permute-done.4 = f32[128,2400]{0,1:T(8,128)} collective-permute-done((f32[128,2400]{0,1:T(8,128)}, f32[128,2400]{0,1:T(8,128)}, u32[]{:S(2)}, u32[]{:S(2)}) %collective-permute-start.4) | collective-permute-done | bytes 1228832 | tf_op jit(solution)/shard_map/ppermute | solution.py:49
  91.1 5.1 %all-to-all-start = ((f32[2,96,512]{2,0,1:T(2,128)}), f32[2,96,512]{2,0,1:T(2,128)S(1)}, u32[]{:S(2)}, u32[]{:S(2)}) async-start(f32[2,96,512]{2,0,1:T(2,128)} %copy.54), calls=%async_computation | async-start | bytes 786432 | tf_op jit(solution)/shard_map/all_to_all | solution.py:29
  96.2 54.0 %all-to-all-done = f32[2,96,512]{2,0,1:T(2,128)S(1)} async-done(((f32[2,96,512]{2,0,1:T(2,128)}), f32[2,96,512]{2,0,1:T(2,128)S(1)}, u32[]{:S(2)}, u32[]{:S(2)}) %all-to-all-start) | async-done | bytes 393248 | tf_op jit(solution)/shard_map/all_to_all | solution.py:29
  150.4 4.8 %fusion.3 = f32[512,2400]{0,1:T(8,128)S(1)} fusion(s32[]{:T(128)S(6)} %select_n.62, f32[128,2400]{0,1:T(8,128)} %collective-permute-done.5, f32[128,2400]{0,1:T(8,128)} %collective-permute-done.4, f32[128,2400]{0,1:T(8,128)} %collective-permute-done.3, f32[128,2400]{0,1:T(8,128)S(1)} %copy-done.9), kind=kLoop, calls=%fused_computation.19 | loop fusion | flops 8601600 | bytes 9830404 | tf_op jit(solution)/shard_map/jit(_roll_dynamic)/concatenate | solution.py:51
  155.2 2.2 copy-done.1
  157.5 3.8 convolution_bitcast_fusion.2
  161.3 3.6 reshape.126
  164.9 7.2 %copy.57 = f32[8,24,3,8,100]{1,4,2,0,3:T(8,128)} copy(f32[8,24,3,8,100]{4,3,2,1,0:T(8,128)} %reshape.126) | data formatting | bytes 3686400 | tf_op jit(solution)/shard_map/reshape | solution.py:64
  172.1 7.5 %reshape.127 = f32[8,24,2400]{2,1,0:T(8,128)} reshape(f32[8,8,3,100,24]{4,3,2,1,0:T(8,128)} %bitcast.75) | data formatting | bytes 3686400 | tf_op jit(solution)/shard_map/reshape | solution.py:65
  179.7 4.3 %all-to-all-start.1 = ((f32[8,24,2400]{2,1,0:T(8,128)}), f32[8,24,2400]{2,1,0:T(8,128)}, u32[]{:S(2)}, u32[]{:S(2)}) async-start(f32[8,24,2400]{2,1,0:T(8,128)} %reshape.127), calls=%async_computation.1 | async-start | bytes 3735552 | tf_op jit(solution)/shard_map/all_to_all | solution.py:66
  186.2 6.2 %convolution_bitcast_fusion.3 = f32[192,2400]{1,0:T(8,128)} fusion(f32[512,2400]{0,1:T(8,128)} %copy-done.1, f32[192,512]{1,0:T(8,128)S(1)} %copy-done.3), kind=kOutput, calls=%fused_computation.33 | convolution fusion | flops 1415577600 | bytes 7151616 | tf_op jit(solution)/shard_map/dot_general | solution.py:61
  192.4 7.1 %fusion.10 = f32[512,2400]{0,1:T(8,128)} fusion(s32[]{:T(128)S(6)} %select_n.62, f32[128,2400]{0,1:T(8,128)} %collective-permute-done.2, f32[128,2400]{0,1:T(8,128)} %collective-permute-done.1, f32[128,2400]{0,1:T(8,128)} %collective-permute-done, f32[128,2400]{0,1:T(8,128)S(1)} %copy-done.8), kind=kLoop, calls=%fused_computation.26 | loop fusion | flops 8601600 | bytes 9830404 | tf_op jit(solution)/shard_map/jit(_roll_dynamic)/concatenate | solution.py:51
  199.5 8.7 %all-to-all-done.1 = f32[8,24,2400]{2,1,0:T(8,128)} async-done(((f32[8,24,2400]{2,1,0:T(8,128)}), f32[8,24,2400]{2,1,0:T(8,128)}, u32[]{:S(2)}, u32[]{:S(2)}) %all-to-all-start.1) | async-done | bytes 1843232 | tf_op jit(solution)/shard_map/all_to_all | solution.py:66
  208.2 5.8 %fusion.32 = f32[192,512]{1,0:T(8,128)} fusion(f32[192,2400]{1,0:T(8,128)} %bitcast.7, f32[2400,512]{1,0:T(8,128)} %bitcast.71), kind=kOutput, calls=%fused_computation.86 | convolution fusion | flops 1415577600 | bytes 7151616 | tf_op jit(solution)/shard_map/dot_general | solution.py:69
  214.0 3.8 convolution_bitcast_fusion
  217.8 3.6 reshape.130
  221.4 7.2 %copy.58 = f32[8,24,3,8,100]{1,4,2,0,3:T(8,128)} copy(f32[8,24,3,8,100]{4,3,2,1,0:T(8,128)} %reshape.130) | data formatting | bytes 3686400 | tf_op jit(solution)/shard_map/reshape | solution.py:64
  228.6 7.5 %reshape.131 = f32[8,24,2400]{2,1,0:T(8,128)} reshape(f32[8,8,3,100,24]{4,3,2,1,0:T(8,128)} %bitcast.76) | data formatting | bytes 3686400 | tf_op jit(solution)/shard_map/reshape | solution.py:65
  236.2 4.3 %all-to-all-start.2 = ((f32[8,24,2400]{2,1,0:T(8,128)}), f32[8,24,2400]{2,1,0:T(8,128)}, u32[]{:S(2)}, u32[]{:S(2)}) async-start(f32[8,24,2400]{2,1,0:T(8,128)} %reshape.131), calls=%async_computation.2 | async-start | bytes 3735552 | tf_op jit(solution)/shard_map/all_to_all | solution.py:66
  240.8 2.5 collective-permute-start.7
  243.3 12.4 %collective-permute-done.9 = f32[128,800]{1,0:T(8,128)S(1)} collective-permute-done((f32[128,800]{1,0:T(8,128)S(1)}, f32[128,800]{1,0:T(8,128)S(1)}, u32[]{:S(2)}, u32[]{:S(2)}) %collective-permute-start.9) | collective-permute-done | bytes 409632 | tf_op jit(solution)/shard_map/ppermute | solution.py:49
  255.7 9.8 %collective-permute-done.7 = f32[128,800]{1,0:T(8,128)S(1)} collective-permute-done((f32[128,800]{1,0:T(8,128)S(1)}, f32[128,800]{1,0:T(8,128)S(1)}, u32[]{:S(2)}, u32[]{:S(2)}) %collective-permute-start.7) | collective-permute-done | bytes 409632 | tf_op jit(solution)/shard_map/ppermute | solution.py:49
  265.5 9.9 %collective-permute-done.10 = f32[128,800]{1,0:T(8,128)} collective-permute-done((f32[128,800]{1,0:T(8,128)S(1)}, f32[128,800]{1,0:T(8,128)}, u32[]{:S(2)}, u32[]{:S(2)}) %collective-permute-start.10) | collective-permute-done | bytes 409632 | tf_op jit(solution)/shard_map/ppermute | solution.py:49
  275.7 9.6 %collective-permute-done.8 = f32[128,800]{1,0:T(8,128)S(1)} collective-permute-done((f32[128,800]{1,0:T(8,128)S(1)}, f32[128,800]{1,0:T(8,128)S(1)}, u32[]{:S(2)}, u32[]{:S(2)}) %collective-permute-start.8) | collective-permute-done | bytes 409632 | tf_op jit(solution)/shard_map/ppermute | solution.py:49
  285.2 2.3 fusion.24
  287.6 6.9 %convolution_bitcast_fusion.1 = f32[192,2400]{1,0:T(8,128)} fusion(f32[512,2400]{0,1:T(8,128)} %fusion.10, f32[192,512]{1,0:T(8,128)S(1)} %copy-done.3), kind=kOutput, calls=%fused_computation.31 | convolution fusion | flops 1415577600 | bytes 7151616 | tf_op jit(solution)/shard_map/dot_general | solution.py:61
  294.4 5.7 %fusion.33 = f32[192,512]{1,0:T(8,128)} fusion(f32[192,2400]{1,0:T(8,128)} %bitcast.13, f32[2400,512]{1,0:T(8,128)} %bitcast.72), kind=kOutput, calls=%fused_computation.87 | convolution fusion | flops 1415577600 | bytes 7151616 | tf_op jit(solution)/shard_map/dot_general | solution.py:69
  302.2 2.2 copy.59
  306.2 4.4 %all-to-all-start.3 = ((f32[8,8,2400]{2,1,0:T(8,128)}), f32[8,8,2400]{2,1,0:T(8,128)S(1)}, u32[]{:S(2)}, u32[]{:S(2)}) async-start(f32[8,8,2400]{2,1,0:T(8,128)} %reshape.134), calls=%async_computation.3 | async-start | bytes 1245184 | tf_op jit(solution)/shard_map/all_to_all | solution.py:66
  310.6 3.1 fusion.17
  313.7 3.2 convolution_bitcast_fusion.7
  316.9 4.4 %all-to-all-done.3 = f32[8,8,2400]{2,1,0:T(8,128)S(1)} async-done(((f32[8,8,2400]{2,1,0:T(8,128)}), f32[8,8,2400]{2,1,0:T(8,128)S(1)}, u32[]{:S(2)}, u32[]{:S(2)}) %all-to-all-start.3) | async-done | bytes 614432 | tf_op jit(solution)/shard_map/all_to_all | solution.py:66
  321.3 4.0 %fusion.28 = f32[64,512]{1,0:T(8,128)S(1)} fusion(f32[2400,512]{1,0:T(8,128)} %bitcast.73, f32[8,8,2400]{2,1,0:T(8,128)S(1)} %all-to-all-done.3), kind=kOutput, calls=%fused_computation.70 | convolution fusion | flops 471859200 | bytes 5660672 | tf_op jit(solution)/shard_map/dot_general | solution.py:69
  328.6 2.4 copy.60
  331.0 3.3 reshape.140
  334.2 3.5 all-to-all-start.4
  339.0 2.0 reshape.137
  341.7 6.8 %all-to-all-done.4 = f32[8,8,2400]{2,1,0:T(8,128)S(1)} async-done(((f32[8,8,2400]{2,1,0:T(8,128)}), f32[8,8,2400]{2,1,0:T(8,128)S(1)}, u32[]{:S(2)}, u32[]{:S(2)}) %all-to-all-start.4) | async-done | bytes 614432 | tf_op jit(solution)/shard_map/all_to_all | solution.py:66
  348.5 4.1 %convolution_bitcast_fusion.8 = f32[8,8,1,512]{3,1,0,2:T(8,128)S(1)} fusion(f32[8,8,2400]{2,1,0:T(8,128)S(1)} %all-to-all-done.4, f32[2400,512,1]{1,0,2:T(8,128)} %bitcast.74), kind=kOutput, calls=%fused_computation.68 | convolution fusion | flops 471859200 | bytes 5660672 | tf_op jit(solution)/shard_map/dot_general | solution.py:69
  353.4 1.7 reshape.141
  355.1 3.1 copy.64
  358.3 2.6 all-to-all-start.5
  363.9 6.6 %concatenate.28 = f32[192,6400]{1,0:T(8,128)} concatenate(f32[192,2400]{1,0:T(8,128)} %convolution_bitcast_fusion.3, f32[192,2400]{1,0:T(8,128)} %convolution_bitcast_fusion.1, f32[192,800]{1,0:T(8,128)} %convolution_bitcast_fusion.7, f32[192,800]{1,0:T(8,128)} %convolution_bitcast_fusion.5), dimensions={1} | concatenate | bytes 9830400 | tf_op jit(solution)/shard_map/concatenate | solution.py:71
  370.5 16.7 %all-to-all-done.5 = f32[32,128,64]{1,2,0:T(8,128)S(1)} async-done(((f32[32,128,64]{1,2,0:T(8,128)}), f32[32,128,64]{1,2,0:T(8,128)S(1)}, u32[]{:S(2)}, u32[]{:S(2)}) %all-to-all-start.5) | async-done | bytes 1048608 | tf_op jit(solution)/shard_map/all_to_all | solution.py:78
  (72 shorter events, 20.8 us)
Async XLA Ops:
  2.7 87.4 %copy-start.3 = (f32[192,512]{1,0:T(8,128)S(1)}, f32[192,512]{1,0:T(8,128)}, u32[]{:S(2)}) copy-start(f32[192,512]{1,0:T(8,128)} %param.9) | copy-start | bytes 1179652
  4.2 33.2 %collective-permute-start.3 = (f32[128,2400]{0,1:T(8,128)}, f32[128,2400]{0,1:T(8,128)}, u32[]{:S(2)}, u32[]{:S(2)}) collective-permute-start(f32[128,2400]{0,1:T(8,128)} %copy.66), channel_id=1, source_target_pairs={{0,1},{1,2},{2,3},{3,0},{4,5},{5,6},{6,7},{7,4},{8,9},{9,10},{10,1... | collective-permute-start | bytes 3686408 | tf_op jit(solution)/shard_map/ppermute | solution.py:49
  7.6 142.7 %copy-start.7 = (f32[128,2400]{0,1:T(8,128)}, f32[128,2400]{0,1:T(8,128)S(1)}, u32[]{:S(2)}) copy-start(f32[128,2400]{0,1:T(8,128)S(1)} %copy.65) | copy-start | bytes 3686404
  7.6 142.8 %copy-start.9 = (f32[128,2400]{0,1:T(8,128)S(1)}, f32[128,2400]{0,1:T(8,128)}, u32[]{:S(2)}) copy-start(f32[128,2400]{0,1:T(8,128)} %copy.66) | copy-start | bytes 3686404
  7.6 56.1 %collective-permute-start = (f32[128,2400]{0,1:T(8,128)S(1)}, f32[128,2400]{0,1:T(8,128)}, u32[]{:S(2)}, u32[]{:S(2)}) collective-permute-start(f32[128,2400]{0,1:T(8,128)S(1)} %copy.65), channel_id=1, source_target_pairs={{0,1},{1,2},{2,3},{3,0},{4,5},{5,6},{6,7},{7,4},{8,9},{9,10},{10,1... | collective-permute-start | bytes 3686408 | tf_op jit(solution)/shard_map/ppermute | solution.py:49
  37.4 52.7 %collective-permute-start.4 = (f32[128,2400]{0,1:T(8,128)}, f32[128,2400]{0,1:T(8,128)}, u32[]{:S(2)}, u32[]{:S(2)}) collective-permute-start(f32[128,2400]{0,1:T(8,128)} %collective-permute-done.3), channel_id=1, source_target_pairs={{0,1},{1,2},{2,3},{3,0},{4,5},{5,6},{6,7},{7,4},{8,9},{9,10},{10,1... | collective-permute-start | bytes 3686408 | tf_op jit(solution)/shard_map/ppermute | solution.py:49
  63.7 86.6 %collective-permute-start.1 = (f32[128,2400]{0,1:T(8,128)}, f32[128,2400]{0,1:T(8,128)}, u32[]{:S(2)}, u32[]{:S(2)}) collective-permute-start(f32[128,2400]{0,1:T(8,128)} %collective-permute-done), channel_id=1, source_target_pairs={{0,1},{1,2},{2,3},{3,0},{4,5},{5,6},{6,7},{7,4},{8,9},{9,10},{10,1... | collective-permute-start | bytes 3686408 | tf_op jit(solution)/shard_map/ppermute | solution.py:49
  90.0 60.4 %collective-permute-start.5 = (f32[128,2400]{0,1:T(8,128)}, f32[128,2400]{0,1:T(8,128)}, u32[]{:S(2)}, u32[]{:S(2)}) collective-permute-start(f32[128,2400]{0,1:T(8,128)} %collective-permute-done.4), channel_id=1, source_target_pairs={{0,1},{1,2},{2,3},{3,0},{4,5},{5,6},{6,7},{7,4},{8,9},{9,10},{10,1... | collective-permute-start | bytes 3686408 | tf_op jit(solution)/shard_map/ppermute | solution.py:49
  91.1 59.1 %all-to-all-start = ((f32[2,96,512]{2,0,1:T(2,128)}), f32[2,96,512]{2,0,1:T(2,128)S(1)}, u32[]{:S(2)}, u32[]{:S(2)}) async-start(f32[2,96,512]{2,0,1:T(2,128)} %copy.54), calls=%async_computation | async-start | bytes 786432 | tf_op jit(solution)/shard_map/all_to_all | solution.py:29
  150.3 149.8 %copy-start.5 = (f32[4,2,24,512]{3,2,1,0:T(8,128)}, f32[4,2,24,512]{3,2,1,0:T(8,128)S(1)}, u32[]{:S(2)}) copy-start(f32[4,2,24,512]{3,2,1,0:T(8,128)S(1)} %copy.56) | copy-start | bytes 1179652
  150.3 42.1 %collective-permute-start.2 = (f32[128,2400]{0,1:T(8,128)}, f32[128,2400]{0,1:T(8,128)}, u32[]{:S(2)}, u32[]{:S(2)}) collective-permute-start(f32[128,2400]{0,1:T(8,128)} %collective-permute-done.1), channel_id=1, source_target_pairs={{0,1},{1,2},{2,3},{3,0},{4,5},{5,6},{6,7},{7,4},{8,9},{9,10},{10,1... | collective-permute-start | bytes 3686408 | tf_op jit(solution)/shard_map/ppermute | solution.py:49
  155.2 2.3 copy-start.1
  179.7 28.5 %all-to-all-start.1 = ((f32[8,24,2400]{2,1,0:T(8,128)}), f32[8,24,2400]{2,1,0:T(8,128)}, u32[]{:S(2)}, u32[]{:S(2)}) async-start(f32[8,24,2400]{2,1,0:T(8,128)} %reshape.127), calls=%async_computation.1 | async-start | bytes 3735552 | tf_op jit(solution)/shard_map/all_to_all | solution.py:66
  185.5 55.0 %copy-start.11 = (f32[128,800]{1,0:T(8,128)}, f32[128,800]{1,0:T(8,128)S(1)}, u32[]{:S(2)}) copy-start(f32[128,800]{1,0:T(8,128)S(1)} %get-tuple-element.22) | copy-start | bytes 1228804
  185.5 6.9 %copy-start.8 = (f32[128,2400]{0,1:T(8,128)S(1)}, f32[128,2400]{0,1:T(8,128)}, u32[]{:S(2)}) copy-start(f32[128,2400]{0,1:T(8,128)} %copy-done.7) | copy-start | bytes 3686404
  185.5 55.3 %collective-permute-start.6 = (f32[128,800]{1,0:T(8,128)S(1)}, f32[128,800]{1,0:T(8,128)S(1)}, u32[]{:S(2)}, u32[]{:S(2)}) collective-permute-start(f32[128,800]{1,0:T(8,128)S(1)} %get-tuple-element.23), channel_id=1, source_target_pairs={{0,1},{1,2},{2,3},{3,0},{4,5},{5,6},{6,7},{7,4},{8,9},{9,10},{10,1... | collective-permute-start | bytes 1228808 | tf_op jit(solution)/shard_map/ppermute | solution.py:49
  208.2 5.8 %copy-start = (f32[512,2400]{0,1:T(8,128)S(1)}, f32[512,2400]{0,1:T(8,128)}, u32[]{:S(2)}) copy-start(f32[512,2400]{0,1:T(8,128)} %fusion.10) | copy-start | bytes 14745604
  236.2 58.2 %all-to-all-start.2 = ((f32[8,24,2400]{2,1,0:T(8,128)}), f32[8,24,2400]{2,1,0:T(8,128)}, u32[]{:S(2)}, u32[]{:S(2)}) async-start(f32[8,24,2400]{2,1,0:T(8,128)} %reshape.131), calls=%async_computation.2 | async-start | bytes 3735552 | tf_op jit(solution)/shard_map/all_to_all | solution.py:66
  240.5 15.2 %collective-permute-start.9 = (f32[128,800]{1,0:T(8,128)S(1)}, f32[128,800]{1,0:T(8,128)S(1)}, u32[]{:S(2)}, u32[]{:S(2)}) collective-permute-start(f32[128,800]{1,0:T(8,128)S(1)} %get-tuple-element.22), channel_id=1, source_target_pairs={{0,1},{1,2},{2,3},{3,0},{4,5},{5,6},{6,7},{7,4},{8,9},{9,10},{10,1... | collective-permute-start | bytes 1228808 | tf_op jit(solution)/shard_map/ppermute | solution.py:49
  240.8 24.8 %collective-permute-start.7 = (f32[128,800]{1,0:T(8,128)S(1)}, f32[128,800]{1,0:T(8,128)S(1)}, u32[]{:S(2)}, u32[]{:S(2)}) collective-permute-start(f32[128,800]{1,0:T(8,128)S(1)} %collective-permute-done.6), channel_id=1, source_target_pairs={{0,1},{1,2},{2,3},{3,0},{4,5},{5,6},{6,7},{7,4},{8,9},{9,10},{10,1... | collective-permute-start | bytes 1228808 | tf_op jit(solution)/shard_map/ppermute | solution.py:49
  255.7 19.9 %copy-start.13 = (f32[128,800]{1,0:T(8,128)}, f32[128,800]{1,0:T(8,128)S(1)}, u32[]{:S(2)}) copy-start(f32[128,800]{1,0:T(8,128)S(1)} %collective-permute-done.9) | copy-start | bytes 1228804
  255.7 19.8 %collective-permute-start.10 = (f32[128,800]{1,0:T(8,128)S(1)}, f32[128,800]{1,0:T(8,128)}, u32[]{:S(2)}, u32[]{:S(2)}) collective-permute-start(f32[128,800]{1,0:T(8,128)S(1)} %collective-permute-done.9), channel_id=1, source_target_pairs={{0,1},{1,2},{2,3},{3,0},{4,5},{5,6},{6,7},{7,4},{8,9},{9,10},{10,1... | collective-permute-start | bytes 1228808 | tf_op jit(solution)/shard_map/ppermute | solution.py:49
  265.5 19.7 %collective-permute-start.8 = (f32[128,800]{1,0:T(8,128)S(1)}, f32[128,800]{1,0:T(8,128)S(1)}, u32[]{:S(2)}, u32[]{:S(2)}) collective-permute-start(f32[128,800]{1,0:T(8,128)S(1)} %collective-permute-done.7), channel_id=1, source_target_pairs={{0,1},{1,2},{2,3},{3,0},{4,5},{5,6},{6,7},{7,4},{8,9},{9,10},{10,1... | collective-permute-start | bytes 1228808 | tf_op jit(solution)/shard_map/ppermute | solution.py:49
  275.5 35.1 %collective-permute-start.11 = (f32[128,800]{1,0:T(8,128)}, f32[128,800]{1,0:T(8,128)}, u32[]{:S(2)}, u32[]{:S(2)}) collective-permute-start(f32[128,800]{1,0:T(8,128)} %collective-permute-done.10), channel_id=1, source_target_pairs={{0,1},{1,2},{2,3},{3,0},{4,5},{5,6},{6,7},{7,4},{8,9},{9,10},{10,1... | collective-permute-start | bytes 1228808 | tf_op jit(solution)/shard_map/ppermute | solution.py:49
  287.5 12.5 %copy-start.2 = (f32[512,800]{1,0:T(8,128)}, f32[512,800]{1,0:T(8,128)S(1)}, u32[]{:S(2)}) copy-start(f32[512,800]{1,0:T(8,128)S(1)} %fusion.24) | copy-start | bytes 4915204
  306.1 7.5 %copy-start.4 = (f32[192,512]{1,0:T(8,128)S(1)}, f32[192,512]{1,0:T(8,128)}, u32[]{:S(2)}) copy-start(f32[192,512]{1,0:T(8,128)} %param.9) | copy-start | bytes 1179652
  306.2 15.2 %all-to-all-start.3 = ((f32[8,8,2400]{2,1,0:T(8,128)}), f32[8,8,2400]{2,1,0:T(8,128)S(1)}, u32[]{:S(2)}, u32[]{:S(2)}) async-start(f32[8,8,2400]{2,1,0:T(8,128)} %reshape.134), calls=%async_computation.3 | async-start | bytes 1245184 | tf_op jit(solution)/shard_map/all_to_all | solution.py:66
  313.7 11.7 %copy-start.6 = (f32[4,2,24,512]{3,2,1,0:T(8,128)S(1)}, f32[4,2,24,512]{3,2,1,0:T(8,128)}, u32[]{:S(2)}) copy-start(f32[4,2,24,512]{3,2,1,0:T(8,128)} %copy-done.5) | copy-start | bytes 1179652
  334.2 14.3 %all-to-all-start.4 = ((f32[8,8,2400]{2,1,0:T(8,128)}), f32[8,8,2400]{2,1,0:T(8,128)S(1)}, u32[]{:S(2)}, u32[]{:S(2)}) async-start(f32[8,8,2400]{2,1,0:T(8,128)} %reshape.140), calls=%async_computation.4 | async-start | bytes 1245184 | tf_op jit(solution)/shard_map/all_to_all | solution.py:66
  341.7 11.1 %copy-start.12 = (f32[8,8,1,512]{3,2,1,0:T(1,128)S(1)}, f32[8,8,1,512]{3,2,1,0:T(1,128)}, u32[]{:S(2)}) copy-start(f32[8,8,1,512]{3,2,1,0:T(1,128)} %copy.61) | copy-start | bytes 393220
  348.5 4.2 %copy-start.10 = (f32[8,8,3,512]{3,2,1,0:T(4,128)S(1)}, f32[8,8,3,512]{3,2,1,0:T(4,128)}, u32[]{:S(2)}) copy-start(f32[8,8,3,512]{3,2,1,0:T(4,128)} %reshape.137) | copy-start | bytes 1179652
  353.4 8.2 %copy-start.14 = (s32[96]{0:T(128)S(1)}, s32[96]{0:T(128)}, u32[]{:S(2)}) copy-start(s32[96]{0:T(128)} %param.12) | copy-start | bytes 1156
  358.3 28.9 %all-to-all-start.5 = ((f32[32,128,64]{1,2,0:T(8,128)}), f32[32,128,64]{1,2,0:T(8,128)S(1)}, u32[]{:S(2)}, u32[]{:S(2)}) async-start(f32[32,128,64]{1,2,0:T(8,128)} %bitcast.27), calls=%async_computation.5 | async-start | bytes 2097152 | tf_op jit(solution)/shard_map/all_to_all | solution.py:78
